TPU v7x, 512 devices: a whole 4x4x16 slice. The times are simulated.
512 devices in a mesh: blk: 32 (over z, core), col: 16 (over y, x).
Axes of the slice: x: 4, y: 4, z: 16, core: 2. Of those that a mesh axis runs over, the one named last changes fastest.
Arguments:
- density: float32 [96, 7, 256, 256], P('blk', None, 'col'), as said below
- band_widths: int32 [96], P('blk'), may hold values from 1 to 3, as said below
Outputs:
- purified: float32 [96, 7, 256, 256], P('blk', None, 'col')
Inputs may be any that keep to these rules, and one draw needn't show every extreme that they name: `band_widths`: each block row keeps between 1 and 3 blocks on each side; 3 is reached in every draw. `density`: diagonal entries of the diagonal blocks lie between 0.05 and 0.95, all other entries are small.
All inputs are finite; a program needn't handle non-finite values.
Results may differ from a plain program's by a relative error of at most 0.00013.
Values sent between devices are 32-bit elements; how exact they have to be, the bound alone decides.
No kernel may reach another device: no remote copies, remote signals or barrier semaphores. Data moves between devices by JAX's collectives and lax.ppermute only.
A program may use at most 64 MiB of HBM per device.

v0:
```python
import jax
import jax.numpy as jnp
from jax import lax
from jax.sharding import PartitionSpec as P

W = 3


def send(cells, shift):
    count = lax.axis_size("blk")
    return lax.ppermute(cells, "blk", [(i, (i + shift) % count) for i in range(count)])


def halo_pieces(cells):
    rows = cells.shape[0]
    tail = [cells[rows - W + k, W - k :] for k in range(W)]
    head = [cells[k, : 2 * W - k] for k in range(W)]
    return (tail, head)


def extend(right):
    tail, head = halo_pieces(right)
    from_left = send(jnp.concatenate(tail, axis=0), 1)
    from_right = send(jnp.concatenate(head, axis=0), -1)
    zero = jnp.zeros((1,) + right.shape[2:], right.dtype)
    rows = []
    start = 0
    for k in range(W):
        width = 2 * W + 1 - (W - k)
        piece = from_left[start : start + width]
        start += width
        rows.append(
            jnp.concatenate([jnp.broadcast_to(zero, (W - k,) + right.shape[2:]), piece], axis=0)
        )
    left = jnp.stack(rows)
    rows = []
    start = 0
    for k in range(W):
        width = 2 * W - k
        piece = from_right[start : start + width]
        start += width
        rows.append(
            jnp.concatenate([piece, jnp.broadcast_to(zero, (k + 1,) + right.shape[2:])], axis=0)
        )
    right_rows = jnp.stack(rows)
    return jnp.concatenate([left, right, right_rows], axis=0)


def contract(extended, shard_rows, keep=None):
    local_rows = shard_rows.shape[0]
    span = 2 * W + 1
    zeros = jnp.zeros_like(extended[:local_rows, :1])
    shifted = []
    for inner_band in range(span):
        window = extended[inner_band : inner_band + local_rows]
        shift = inner_band - W
        if shift > 0:
            window = jnp.concatenate([zeros] * shift + [window[:, : span - shift]], axis=1)
        elif shift < 0:
            window = jnp.concatenate([window[:, -shift:]] + [zeros] * -shift, axis=1)
        shifted.append(window)
    stacked = jnp.stack(shifted, axis=3)
    if keep is not None:
        shard_rows = shard_rows * keep
    return jnp.einsum("ibcas,iasr->ibcr", stacked, shard_rows, precision=lax.Precision.HIGH)


def on_device(density, band_widths):
    offsets = jnp.abs(jnp.arange(2 * W + 1, dtype=jnp.int32) - W)
    pattern = (offsets[None, :] <= band_widths[:, None]).astype(jnp.float32)[:, :, None, None]
    current = density * pattern
    for purify_step in range(2):
        if purify_step == 0:
            gathered, keep = (lax.all_gather(density, "col", axis=2, tiled=True), pattern)
        else:
            gathered, keep = (lax.all_gather(current, "col", axis=2, tiled=True), None)
        square = contract(extend(current), gathered, keep) * pattern
        third_power = contract(extend(square), gathered, keep) * pattern
        current = 3.0 * square - 2.0 * third_power
    return current


def solution(mesh):
    in_specs = (P("blk", None, "col", None), P("blk"))
    out_specs = P("blk", None, "col", None)
    return jax.shard_map(
        on_device, mesh=mesh, in_specs=in_specs, out_specs=out_specs, check_vma=False
    )
```

profile of v0, /device:TPU:97, one launch (start us, length us, event | category | flops | bytes accessed | tf_op | source)
XLA Modules:
  0.0 198.5 jit_solution(10707903417032842990)
XLA Ops:
  6.5 0.0 all-gather.3.cloned.1.call-start
  6.5 0.7 all-gather.3.cloned.1.call-update
  7.3 0.0 all-gather.5.cloned.1.call-start
  7.3 0.7 compare_convert_fusion
  8.0 1.1 broadcast_multiply_fusion
  9.2 0.0 copy-start.2
  9.2 3.4 %collective-permute-start = (f32[15,16,256]{2,1,0:T(8,128)S(1)}, f32[15,16,256]{2,1,0:T(8,128)S(1)}, u32[]{:S(2)}, u32[]{:S(2)}) collective-permute-start(f32[15,16,256]{2,1,0:T(8,128)S(1)} %pad_maximum_fusion), channel_id=1, source_target_pairs={{0,16},{16,32},{32,48},{48,64},{64,80},{80,96},{96,112},{112,128},... | collective-permute-start | bytes 737288 | tf_op jit(solution)/shard_map/ppermute | solution.py:11
  12.7 0.0 collective-permute-start.1
  12.7 3.1 %collective-permute-done = f32[15,16,256]{2,1,0:T(8,128)S(1)} collective-permute-done((f32[15,16,256]{2,1,0:T(8,128)S(1)}, f32[15,16,256]{2,1,0:T(8,128)S(1)}, u32[]{:S(2)}, u32[]{:S(2)}) %collective-permute-start) | collective-permute-done | bytes 245792 | tf_op jit(solution)/shard_map/ppermute | solution.py:11
  15.8 3.7 %collective-permute-done.1 = f32[15,16,256]{2,1,0:T(8,128)S(1)} collective-permute-done((f32[15,16,256]{2,1,0:T(8,128)S(1)}, f32[15,16,256]{2,1,0:T(8,128)S(1)}, u32[]{:S(2)}, u32[]{:S(2)}) %collective-permute-start.1) | collective-permute-done | bytes 245792 | tf_op jit(solution)/shard_map/ppermute | solution.py:11
  19.7 0.0 copy-done.2
  19.7 0.1 fusion.84
  19.8 0.0 copy-done.1
  19.8 0.1 bitcast_dynamic-update-slice_fusion
  20.0 66.8 %all-gather.3.cloned.1.call-done = f32[3,7,256,256]{3,2,1,0:T(8,128)} async-done(((f32[3,7,16,256]{3,2,1,0:T(8,128)}), f32[3,7,256,256]{3,2,1,0:T(8,128)}) %all-gather.3.cloned.1.call-update) | async-done | bytes 5505040 | tf_op jit(solution)/shard_map/all_gather | solution.py:74
  86.8 4.4 %fusion.16 = f32[3,7,16,256]{3,2,1,0:T(8,128)S(1)} fusion(f32[3,7,16,7,256]{4,2,3,1,0:T(8,128)S(1)} %fusion.68, f32[3,7,256,256]{3,2,1,0:T(8,128)} %all-gather.3.cloned.1.call-done, f32[3,7]{1,0:T(4,128)S(1)} %compare_convert_fusion), kind=kOutput, calls=%fused_computation.15 | convolution fusion | flops 926306304 | bytes 8257620 | tf_op jit(solution)/shard_map/ibcas,iasr->ibcr/dot_general | solution.py:65
  91.2 0.0 slice-start.1
  91.3 3.1 %collective-permute-start.2 = (f32[15,16,256]{2,1,0:T(8,128)S(1)}, f32[15,16,256]{2,1,0:T(8,128)S(1)}, u32[]{:S(2)}, u32[]{:S(2)}) collective-permute-start(f32[15,16,256]{2,1,0:T(8,128)S(1)} %pad_maximum_fusion.2), channel_id=1, source_target_pairs={{0,16},{16,32},{32,48},{48,64},{64,80},{80,96},{96,112},{112,128},... | collective-permute-start | bytes 737288 | tf_op jit(solution)/shard_map/ppermute | solution.py:11
  94.4 0.0 collective-permute-start.3
  94.4 3.1 %collective-permute-done.2 = f32[15,16,256]{2,1,0:T(8,128)S(1)} collective-permute-done((f32[15,16,256]{2,1,0:T(8,128)S(1)}, f32[15,16,256]{2,1,0:T(8,128)S(1)}, u32[]{:S(2)}, u32[]{:S(2)}) %collective-permute-start.2) | collective-permute-done | bytes 245792 | tf_op jit(solution)/shard_map/ppermute | solution.py:11
  97.7 3.5 %collective-permute-done.3 = f32[15,16,256]{2,1,0:T(8,128)S(1)} collective-permute-done((f32[15,16,256]{2,1,0:T(8,128)S(1)}, f32[15,16,256]{2,1,0:T(8,128)S(1)}, u32[]{:S(2)}, u32[]{:S(2)}) %collective-permute-start.3) | collective-permute-done | bytes 245792 | tf_op jit(solution)/shard_map/ppermute | solution.py:11
  101.3 0.1 fusion.83
  101.4 0.0 slice-done
  101.5 0.0 slice-done.1
  101.5 1.7 fusion.2
  103.2 0.8 fusion.80
  104.0 0.0 all-gather.5.cloned.1.call-update
  104.0 0.9 slice_bitcast_fusion.18
  105.0 1.0 slice_bitcast_fusion.10
  106.0 1.0 slice_bitcast_fusion.2
  106.9 0.2 collective-permute-start.4
  107.2 0.3 collective-permute-start.5
  107.5 2.8 %collective-permute-done.4 = f32[15,16,256]{2,1,0:T(8,128)S(1)} collective-permute-done((f32[15,16,256]{2,1,0:T(8,128)S(1)}, f32[15,16,256]{2,1,0:T(8,128)S(1)}, u32[]{:S(2)}, u32[]{:S(2)}) %collective-permute-start.4) | collective-permute-done | bytes 245792 | tf_op jit(solution)/shard_map/ppermute | solution.py:11
  110.3 3.7 %collective-permute-done.5 = f32[15,16,256]{2,1,0:T(8,128)S(1)} collective-permute-done((f32[15,16,256]{2,1,0:T(8,128)S(1)}, f32[15,16,256]{2,1,0:T(8,128)S(1)}, u32[]{:S(2)}, u32[]{:S(2)}) %collective-permute-start.5) | collective-permute-done | bytes 245792 | tf_op jit(solution)/shard_map/ppermute | solution.py:11
  114.2 0.0 copy-done
  114.2 0.1 fusion.82
  114.4 59.8 %all-gather.5.cloned.1.call-done = f32[3,7,256,256]{3,2,1,0:T(8,128)} async-done(((f32[3,7,16,256]{3,2,1,0:T(8,128)}), f32[3,7,256,256]{3,2,1,0:T(8,128)}) %all-gather.5.cloned.1.call-update) | async-done | bytes 5505040 | tf_op jit(solution)/shard_map/all_gather | solution.py:76
  174.2 4.4 %fusion.6 = f32[3,7,16,256,1]{3,2,0,1,4:T(8,128)S(1)} fusion(f32[3,7,16,7,256]{4,2,1,0,3:T(8,128)S(1)} %fusion.32, f32[3,7,256,256]{3,2,1,0:T(8,128)} %all-gather.5.cloned.1.call-done), kind=kOutput, calls=%fused_computation.6 | convolution fusion | flops 924844032 | bytes 8257536 | tf_op jit(solution)/shard_map/ibcas,iasr->ibcr/dot_general | solution.py:65
  178.7 0.1 bitcast_multiply_fusion.1
  178.8 0.0 slice-start.3
  178.9 3.1 %collective-permute-start.6 = (f32[15,16,256]{2,1,0:T(8,128)S(1)}, f32[15,16,256]{2,1,0:T(8,128)S(1)}, u32[]{:S(2)}, u32[]{:S(2)}) collective-permute-start(f32[15,16,256]{2,1,0:T(8,128)S(1)} %pad_maximum_fusion.6), channel_id=1, source_target_pairs={{0,16},{16,32},{32,48},{48,64},{64,80},{80,96},{96,112},{112,128},... | collective-permute-start | bytes 737288 | tf_op jit(solution)/shard_map/ppermute | solution.py:11
  181.9 0.0 collective-permute-start.7
  182.0 3.1 %collective-permute-done.6 = f32[15,16,256]{2,1,0:T(8,128)S(1)} collective-permute-done((f32[15,16,256]{2,1,0:T(8,128)S(1)}, f32[15,16,256]{2,1,0:T(8,128)S(1)}, u32[]{:S(2)}, u32[]{:S(2)}) %collective-permute-start.6) | collective-permute-done | bytes 245792 | tf_op jit(solution)/shard_map/ppermute | solution.py:11
  185.2 0.1 bitcast_dynamic-update-slice_fusion.1
  185.3 3.4 %collective-permute-done.7 = f32[15,16,256]{2,1,0:T(8,128)S(1)} collective-permute-done((f32[15,16,256]{2,1,0:T(8,128)S(1)}, f32[15,16,256]{2,1,0:T(8,128)S(1)}, u32[]{:S(2)}, u32[]{:S(2)}) %collective-permute-start.7) | collective-permute-done | bytes 245792 | tf_op jit(solution)/shard_map/ppermute | solution.py:11
  188.8 0.1 fusion.81
  189.0 1.8 fusion.4
  190.8 0.9 fusion.78
  (90 shorter events, 1.2 us)
Async XLA Ops:
  6.5 80.2 %all-gather.3.cloned.1.call-start = ((), (), s32[]{:S(2)}) async-start(), calls=%async_computation | async-start | bytes 5849088 | tf_op jit(solution)/shard_map/all_gather | solution.py:74
  7.3 167.0 %all-gather.5.cloned.1.call-start = ((), (), s32[]{:S(2)}) async-start(), calls=%async_computation.1 | async-start | bytes 5849088 | tf_op jit(solution)/shard_map/all_gather | solution.py:76
  9.2 10.5 %copy-start.2 = (pred[7]{0:T(512)(128)(4,1)S(1)}, pred[7]{0:T(512)(128)(4,1)}, u32[]{:S(2)}) copy-start(pred[7]{0:T(512)(128)(4,1)} %constant.7.clone.1) | copy-start | bytes 25
  9.2 6.6 %collective-permute-start = (f32[15,16,256]{2,1,0:T(8,128)S(1)}, f32[15,16,256]{2,1,0:T(8,128)S(1)}, u32[]{:S(2)}, u32[]{:S(2)}) collective-permute-start(f32[15,16,256]{2,1,0:T(8,128)S(1)} %pad_maximum_fusion), channel_id=1, source_target_pairs={{0,16},{16,32},{32,48},{48,64},{64,80},{80,96},{96,112},{112,128},... | collective-permute-start | bytes 737288 | tf_op jit(solution)/shard_map/ppermute | solution.py:11
  12.6 7.1 %copy-start.1 = (f32[3,7,16,256]{3,2,1,0:T(8,128)S(1)}, f32[3,7,16,256]{3,2,1,0:T(8,128)}, u32[]{:S(2)}) copy-start(f32[3,7,16,256]{3,2,1,0:T(8,128)} %param.2) | copy-start | bytes 1032196
  12.7 6.8 %collective-permute-start.1 = (f32[15,16,256]{2,1,0:T(8,128)S(1)}, f32[15,16,256]{2,1,0:T(8,128)S(1)}, u32[]{:S(2)}, u32[]{:S(2)}) collective-permute-start(f32[15,16,256]{2,1,0:T(8,128)S(1)} %pad_maximum_fusion.1), channel_id=1, source_target_pairs={{0,496},{16,0},{32,16},{48,32},{64,48},{80,64},{96,80},{112,96},{1... | collective-permute-start | bytes 737288 | tf_op jit(solution)/shard_map/ppermute | solution.py:11
  86.8 14.7 %slice-start = ((s8[5505024]{0:T(1024)(128)(4,1)}), s8[4194304]{0:T(1024)(128)(4,1)S(1)}, s32[]{:S(2)}) async-start(s8[5505024]{0:T(1024)(128)(4,1)} %bitcast.255), calls=%async_computation.2 | async-start | bytes 8388608
  91.2 10.2 %slice-start.1 = ((s8[5505024]{0:T(1024)(128)(4,1)}), s8[1310720]{0:T(1024)(128)(4,1)S(1)}, s32[]{:S(2)}) async-start(s8[5505024]{0:T(1024)(128)(4,1)} %bitcast.255), calls=%async_computation.3 | async-start | bytes 2621440
  91.3 6.2 %collective-permute-start.2 = (f32[15,16,256]{2,1,0:T(8,128)S(1)}, f32[15,16,256]{2,1,0:T(8,128)S(1)}, u32[]{:S(2)}, u32[]{:S(2)}) collective-permute-start(f32[15,16,256]{2,1,0:T(8,128)S(1)} %pad_maximum_fusion.2), channel_id=1, source_target_pairs={{0,16},{16,32},{32,48},{48,64},{64,80},{80,96},{96,112},{112,128},... | collective-permute-start | bytes 737288 | tf_op jit(solution)/shard_map/ppermute | solution.py:11
  94.4 6.8 %collective-permute-start.3 = (f32[15,16,256]{2,1,0:T(8,128)S(1)}, f32[15,16,256]{2,1,0:T(8,128)S(1)}, u32[]{:S(2)}, u32[]{:S(2)}) collective-permute-start(f32[15,16,256]{2,1,0:T(8,128)S(1)} %pad_maximum_fusion.3), channel_id=1, source_target_pairs={{0,496},{16,0},{32,16},{48,32},{64,48},{80,64},{96,80},{112,96},{1... | collective-permute-start | bytes 737288 | tf_op jit(solution)/shard_map/ppermute | solution.py:11
  104.0 10.1 %copy-start = (f32[3,7,16,256]{3,2,1,0:T(8,128)S(1)}, f32[3,7,16,256]{3,2,1,0:T(8,128)}, u32[]{:S(2)}) copy-start(f32[3,7,16,256]{3,2,1,0:T(8,128)} %fusion.80) | copy-start | bytes 1032196
  106.9 3.4 %collective-permute-start.4 = (f32[15,16,256]{2,1,0:T(8,128)S(1)}, f32[15,16,256]{2,1,0:T(8,128)S(1)}, u32[]{:S(2)}, u32[]{:S(2)}) collective-permute-start(f32[15,16,256]{2,1,0:T(8,128)S(1)} %pad_maximum_fusion.4), channel_id=1, source_target_pairs={{0,16},{16,32},{32,48},{48,64},{64,80},{80,96},{96,112},{112,128},... | collective-permute-start | bytes 737288 | tf_op jit(solution)/shard_map/ppermute | solution.py:11
  107.2 6.8 %collective-permute-start.5 = (f32[15,16,256]{2,1,0:T(8,128)S(1)}, f32[15,16,256]{2,1,0:T(8,128)S(1)}, u32[]{:S(2)}, u32[]{:S(2)}) collective-permute-start(f32[15,16,256]{2,1,0:T(8,128)S(1)} %pad_maximum_fusion.5), channel_id=1, source_target_pairs={{0,496},{16,0},{32,16},{48,32},{64,48},{80,64},{96,80},{112,96},{1... | collective-permute-start | bytes 737288 | tf_op jit(solution)/shard_map/ppermute | solution.py:11
  174.2 14.8 %slice-start.2 = ((s8[5505024]{0:T(1024)(128)(4,1)}), s8[4194304]{0:T(1024)(128)(4,1)S(1)}, s32[]{:S(2)}) async-start(s8[5505024]{0:T(1024)(128)(4,1)} %bitcast.257), calls=%async_computation.4 | async-start | bytes 8388608
  178.8 10.3 %slice-start.3 = ((s8[5505024]{0:T(1024)(128)(4,1)}), s8[1310720]{0:T(1024)(128)(4,1)S(1)}, s32[]{:S(2)}) async-start(s8[5505024]{0:T(1024)(128)(4,1)} %bitcast.257), calls=%async_computation.5 | async-start | bytes 2621440
  178.9 6.2 %collective-permute-start.6 = (f32[15,16,256]{2,1,0:T(8,128)S(1)}, f32[15,16,256]{2,1,0:T(8,128)S(1)}, u32[]{:S(2)}, u32[]{:S(2)}) collective-permute-start(f32[15,16,256]{2,1,0:T(8,128)S(1)} %pad_maximum_fusion.6), channel_id=1, source_target_pairs={{0,16},{16,32},{32,48},{48,64},{64,80},{80,96},{96,112},{112,128},... | collective-permute-start | bytes 737288 | tf_op jit(solution)/shard_map/ppermute | solution.py:11
  181.9 6.8 %collective-permute-start.7 = (f32[15,16,256]{2,1,0:T(8,128)S(1)}, f32[15,16,256]{2,1,0:T(8,128)S(1)}, u32[]{:S(2)}, u32[]{:S(2)}) collective-permute-start(f32[15,16,256]{2,1,0:T(8,128)S(1)} %pad_maximum_fusion.7), channel_id=1, source_target_pairs={{0,496},{16,0},{32,16},{48,32},{64,48},{80,64},{96,80},{112,96},{1... | collective-permute-start | bytes 737288 | tf_op jit(solution)/shard_map/ppermute | solution.py:11
Sparse Core Ops, SparseCore 0:
  10.4 76.3 all-gather.2
  104.2 70.0 all-gather.4
where the time goes:
time: 199 us; the launch traced here: 198 us
  waiting for transfers between devices  154 us (77%)
  between operations  14.1 us (7%)
  matrix products  12.3 us (6%)
  starting transfers between devices  10.2 us (5%)
  other arithmetic  4.81 us (2%)
  local copies, waits for them, and re-layouts  3.36 us (2%)
    all_gather x1, waiting for transfers between devices, on_device(): lax.all_gather(density, 'col', axis=2, tiled=True)  66.8 us
    all_gather x1, waiting for transfers between devices, on_device(): gathered, keep = (lax.all_gather(current, 'col', axis=2, tiled=True), None)  59.8 us
    ppermute x8, waiting for transfers between devices, send(): lax.ppermute(cells, 'blk', [(i, (i + shift) % count) for i in range(count)])  26.4 us
    dot_general x4, matrix products, contract(): jnp.einsum('ibcas,iasr->ibcr', stacked, shard_rows, precision=lax.Precisi...  12.3 us
    ppermute x8, starting transfers between devices, send(): lax.ppermute(cells, 'blk', [(i, (i + shift) % count) for i in range(count)])  10.1 us
  transfers between devices with their start and end apart: 10, of which 10 were waited for; matrix products, arithmetic and copies ran while one was open for 3% of the time, Pallas kernels for 0%

commit v1 on v0

--- a/solution.py
+++ b/solution.py
@@ -4,6 +4,27 @@
 from jax.sharding import PartitionSpec as P
 
 W = 3
+
+
+def collect(x, axis, dim):
+    peers, mine, rows = (lax.axis_size(axis), lax.axis_index(axis), x.shape[dim])
+    right = [(i, (i + 1) % peers) for i in range(peers)]
+    left = [(i, (i - 1) % peers) for i in range(peers)]
+    filled = jnp.zeros((*x.shape[:dim], peers * rows, *x.shape[dim + 1 :]), x.dtype)
+    filled = lax.dynamic_update_slice_in_dim(filled, x, mine * rows, axis=dim)
+    from_left = from_right = x
+    half = peers // 2
+    for turn in range(1, half + 1):
+        from_left = lax.ppermute(from_left, axis, right)
+        filled = lax.dynamic_update_slice_in_dim(
+            filled, from_left, (mine - turn) % peers * rows, axis=dim
+        )
+        if turn < peers - half:
+            from_right = lax.ppermute(from_right, axis, left)
+            filled = lax.dynamic_update_slice_in_dim(
+                filled, from_right, (mine + turn) % peers * rows, axis=dim
+            )
+    return filled
 
 
 def send(cells, shift):
@@ -71,7 +92,7 @@
     current = density * pattern
     for purify_step in range(2):
         if purify_step == 0:
-            gathered, keep = (lax.all_gather(density, "col", axis=2, tiled=True), pattern)
+            gathered, keep = (collect(density, "col", 2), pattern)
         else:
             gathered, keep = (lax.all_gather(current, "col", axis=2, tiled=True), None)
         square = contract(extend(current), gathered, keep) * pattern

time: 199 us -> 234 us (1.18)
  starting transfers between devices: 10.2 us -> 76.1 us
  waiting for transfers between devices: 154 us -> 106 us
  local copies, waits for them, and re-layouts: 3.36 us -> 18.1 us
  matrix products: 12.3 us -> 14.7 us
    all_gather x1 -> x0, waiting for transfers between devices: 66.8 us -> none  [on_device(): lax.all_gather(density, 'col', axis=2, tiled=True)]
    ppermute x0 -> x15, starting transfers between devices: none -> 62.1 us  [the longest x7 45.4 us: collect(): from_right = lax.ppermute(from_right, axis, left)]
    ppermute x0 -> x15, waiting for transfers between devices: none -> 30 us  [the longest x8 29.9 us: collect(): from_left = lax.ppermute(from_left, axis, right)]
    dynamic_update_slice x0 -> x15, local copies, waits for them, and re-layouts: none -> 11.7 us  [the longest x8 6.22 us: collect(): lax.dynamic_update_slice_in_dim(filled, from_left, (mine - turn) % peers...]
    ppermute x8, waiting for transfers between devices: 26.4 us -> 20.6 us  [send(): lax.ppermute(cells, 'blk', [(i, (i + shift) % count) for i in range(count)])]
    all_gather x1, waiting for transfers between devices: 59.8 us -> 55.2 us  [on_device(): gathered, keep = (lax.all_gather(current, 'col', axis=2, tiled=True), None)]
    ppermute x8, starting transfers between devices: 10.1 us -> 14 us  [send(): lax.ppermute(cells, 'blk', [(i, (i + shift) % count) for i in range(count)])]
    broadcast_in_dim x0 -> x1, local copies, waits for them, and re-layouts: none -> 3.02 us  [collect(): jnp.zeros((*x.shape[:dim], peers * rows, *x.shape[dim + 1:]), x.dtype)]
  transfers between devices with their start and end apart: 10 -> 24, of which waited for: 10 -> 17; matrix products, arithmetic and copies ran while one was open for 3% -> 6% of each run, Pallas kernels for 0% -> 0%
where the time goes in v1:
time: 234 us
  waiting for transfers between devices  106 us (45%)
  starting transfers between devices  76.1 us (33%)
  local copies, waits for them, and re-layouts  18.1 us (8%)
  matrix products  14.7 us (6%)
  between operations  14.5 us (6%)
  other arithmetic  4.52 us (2%)
    all_gather x1, waiting for transfers between devices, on_device(): gathered, keep = (lax.all_gather(current, 'col', axis=2, tiled=True), None)  55.2 us
    ppermute x7, starting transfers between devices, collect(): from_right = lax.ppermute(from_right, axis, left)  45.4 us
    ppermute x8, waiting for transfers between devices, collect(): from_left = lax.ppermute(from_left, axis, right)  29.9 us
    ppermute x8, waiting for transfers between devices, send(): lax.ppermute(cells, 'blk', [(i, (i + shift) % count) for i in range(count)])  20.6 us
    ppermute x8, starting transfers between devices, collect(): from_left = lax.ppermute(from_left, axis, right)  16.6 us
    dot_general x4, matrix products, contract(): jnp.einsum('ibcas,iasr->ibcr', stacked, shard_rows, precision=lax.Precisi...  14.7 us
    ppermute x8, starting transfers between devices, send(): lax.ppermute(cells, 'blk', [(i, (i + shift) % count) for i in range(count)])  14 us
    dynamic_update_slice x8, local copies, waits for them, and re-layouts, collect(): lax.dynamic_update_slice_in_dim(filled, from_left, (mine - turn) % peers...  6.22 us
  transfers between devices with their start and end apart: 24, of which 17 were waited for; matrix products, arithmetic and copies ran while one was open for 6% of the time, Pallas kernels for 0%

profile of v1, /device:TPU:97, one launch (start us, length us, event | category | flops | bytes accessed | tf_op | source)
XLA Modules:
  0.0 233.7 jit_solution(14194893266792425303)
XLA Ops:
  7.3 3.0 %broadcast_in_dim.2 = f32[3,7,256,256]{3,2,1,0:T(8,128)} broadcast(f32[]{:T(128)} %constant.103.clone.1), dimensions={} | broadcast | bytes 5505028 | tf_op jit(solution)/shard_map/broadcast_in_dim | solution.py:13
  10.3 0.9 broadcast_multiply_fusion
  11.2 3.4 %collective-permute-start = (f32[15,16,256]{2,1,0:T(8,128)S(1)}, f32[15,16,256]{2,1,0:T(8,128)S(1)}, u32[]{:S(2)}, u32[]{:S(2)}) collective-permute-start(f32[15,16,256]{2,1,0:T(8,128)S(1)} %pad_maximum_fusion), channel_id=1, source_target_pairs={{0,16},{16,32},{32,48},{48,64},{64,80},{80,96},{96,112},{112,128},... | collective-permute-start | bytes 737288 | tf_op jit(solution)/shard_map/ppermute | solution.py:32
  14.7 3.1 %collective-permute-start.2 = (f32[3,7,16,256]{3,2,1,0:T(8,128)S(1)}, f32[3,7,16,256]{3,2,1,0:T(8,128)S(1)}, u32[]{:S(2)}, u32[]{:S(2)}) collective-permute-start(f32[3,7,16,256]{3,2,1,0:T(8,128)S(1)} %copy-done.1), channel_id=1, source_target_pairs={{0,1},{1,2},{2,3},{3,4},{4,5},{5,6},{6,7},{7,8},{8,9},{9,10},{10,1... | collective-permute-start | bytes 1032200 | tf_op jit(solution)/shard_map/ppermute | solution.py:18
  17.8 5.6 %collective-permute-start.3 = (f32[3,7,16,256]{3,2,1,0:T(8,128)S(1)}, f32[3,7,16,256]{3,2,1,0:T(8,128)S(1)}, u32[]{:S(2)}, u32[]{:S(2)}) collective-permute-start(f32[3,7,16,256]{3,2,1,0:T(8,128)S(1)} %copy-done.1), channel_id=1, source_target_pairs={{0,15},{1,0},{2,1},{3,2},{4,3},{5,4},{6,5},{7,6},{8,7},{9,8},{10,9... | collective-permute-start | bytes 1032200 | tf_op jit(solution)/shard_map/ppermute | solution.py:23
  23.9 3.5 %collective-permute-done.2 = f32[3,7,16,256]{3,2,1,0:T(8,128)S(1)} collective-permute-done((f32[3,7,16,256]{3,2,1,0:T(8,128)S(1)}, f32[3,7,16,256]{3,2,1,0:T(8,128)S(1)}, u32[]{:S(2)}, u32[]{:S(2)}) %collective-permute-start.2) | collective-permute-done | bytes 344096 | tf_op jit(solution)/shard_map/ppermute | solution.py:18
  27.4 1.9 collective-permute-start.4
  29.4 0.9 collective-permute-done.1
  30.3 6.0 %collective-permute-start.5 = (f32[3,7,16,256]{3,2,1,0:T(8,128)S(1)}, f32[3,7,16,256]{3,2,1,0:T(8,128)S(1)}, u32[]{:S(2)}, u32[]{:S(2)}) collective-permute-start(f32[3,7,16,256]{3,2,1,0:T(8,128)S(1)} %collective-permute-done.3), channel_id=1, source_target_pairs={{0,15},{1,0},{2,1},{3,2},{4,3},{5,4},{6,5},{7,6},{8,7},{9,8},{10,9... | collective-permute-start | bytes 1032200 | tf_op jit(solution)/shard_map/ppermute | solution.py:23
  36.4 4.7 %collective-permute-done.4 = f32[3,7,16,256]{3,2,1,0:T(8,128)S(1)} collective-permute-done((f32[3,7,16,256]{3,2,1,0:T(8,128)S(1)}, f32[3,7,16,256]{3,2,1,0:T(8,128)S(1)}, u32[]{:S(2)}, u32[]{:S(2)}) %collective-permute-start.4) | collective-permute-done | bytes 344096 | tf_op jit(solution)/shard_map/ppermute | solution.py:18
  41.1 1.9 collective-permute-start.6
  43.1 7.1 %collective-permute-start.7 = (f32[3,7,16,256]{3,2,1,0:T(8,128)S(1)}, f32[3,7,16,256]{3,2,1,0:T(8,128)S(1)}, u32[]{:S(2)}, u32[]{:S(2)}) collective-permute-start(f32[3,7,16,256]{3,2,1,0:T(8,128)S(1)} %collective-permute-done.5), channel_id=1, source_target_pairs={{0,15},{1,0},{2,1},{3,2},{4,3},{5,4},{6,5},{7,6},{8,7},{9,8},{10,9... | collective-permute-start | bytes 1032200 | tf_op jit(solution)/shard_map/ppermute | solution.py:23
  50.3 5.7 %collective-permute-done.6 = f32[3,7,16,256]{3,2,1,0:T(8,128)S(1)} collective-permute-done((f32[3,7,16,256]{3,2,1,0:T(8,128)S(1)}, f32[3,7,16,256]{3,2,1,0:T(8,128)S(1)}, u32[]{:S(2)}, u32[]{:S(2)}) %collective-permute-start.6) | collective-permute-done | bytes 344096 | tf_op jit(solution)/shard_map/ppermute | solution.py:18
  56.0 1.9 collective-permute-start.8
  58.7 6.7 %collective-permute-start.9 = (f32[3,7,16,256]{3,2,1,0:T(8,128)S(1)}, f32[3,7,16,256]{3,2,1,0:T(8,128)S(1)}, u32[]{:S(2)}, u32[]{:S(2)}) collective-permute-start(f32[3,7,16,256]{3,2,1,0:T(8,128)S(1)} %collective-permute-done.7), channel_id=1, source_target_pairs={{0,15},{1,0},{2,1},{3,2},{4,3},{5,4},{6,5},{7,6},{8,7},{9,8},{10,9... | collective-permute-start | bytes 1032200 | tf_op jit(solution)/shard_map/ppermute | solution.py:23
  65.4 0.8 constant_dynamic-update-slice_fusion.13
  66.2 4.2 %collective-permute-done.8 = f32[3,7,16,256]{3,2,1,0:T(8,128)S(1)} collective-permute-done((f32[3,7,16,256]{3,2,1,0:T(8,128)S(1)}, f32[3,7,16,256]{3,2,1,0:T(8,128)S(1)}, u32[]{:S(2)}, u32[]{:S(2)}) %collective-permute-start.8) | collective-permute-done | bytes 344096 | tf_op jit(solution)/shard_map/ppermute | solution.py:18
  70.4 1.9 collective-permute-start.10
  72.3 0.8 constant_dynamic-update-slice_fusion.12
  73.9 6.7 %collective-permute-start.11 = (f32[3,7,16,256]{3,2,1,0:T(8,128)S(1)}, f32[3,7,16,256]{3,2,1,0:T(8,128)S(1)}, u32[]{:S(2)}, u32[]{:S(2)}) collective-permute-start(f32[3,7,16,256]{3,2,1,0:T(8,128)S(1)} %collective-permute-done.9), channel_id=1, source_target_pairs={{0,15},{1,0},{2,1},{3,2},{4,3},{5,4},{6,5},{7,6},{8,7},{9,8},{10,9... | collective-permute-start | bytes 1032200 | tf_op jit(solution)/shard_map/ppermute | solution.py:23
  81.4 2.6 %collective-permute-done.10 = f32[3,7,16,256]{3,2,1,0:T(8,128)S(1)} collective-permute-done((f32[3,7,16,256]{3,2,1,0:T(8,128)S(1)}, f32[3,7,16,256]{3,2,1,0:T(8,128)S(1)}, u32[]{:S(2)}, u32[]{:S(2)}) %collective-permute-start.10) | collective-permute-done | bytes 344096 | tf_op jit(solution)/shard_map/ppermute | solution.py:18
  83.9 1.9 collective-permute-start.12
  85.9 0.8 constant_dynamic-update-slice_fusion.9
  87.4 6.7 %collective-permute-start.13 = (f32[3,7,16,256]{3,2,1,0:T(8,128)S(1)}, f32[3,7,16,256]{3,2,1,0:T(8,128)S(1)}, u32[]{:S(2)}, u32[]{:S(2)}) collective-permute-start(f32[3,7,16,256]{3,2,1,0:T(8,128)S(1)} %collective-permute-done.11), channel_id=1, source_target_pairs={{0,15},{1,0},{2,1},{3,2},{4,3},{5,4},{6,5},{7,6},{8,7},{9,8},{10,9... | collective-permute-start | bytes 1032200 | tf_op jit(solution)/shard_map/ppermute | solution.py:23
  94.9 1.7 collective-permute-done.12
  96.5 1.9 collective-permute-start.14
  100.0 6.7 %collective-permute-start.15 = (f32[3,7,16,256]{3,2,1,0:T(8,128)S(1)}, f32[3,7,16,256]{3,2,1,0:T(8,128)S(1)}, u32[]{:S(2)}, u32[]{:S(2)}) collective-permute-start(f32[3,7,16,256]{3,2,1,0:T(8,128)S(1)} %collective-permute-done.13), channel_id=1, source_target_pairs={{0,15},{1,0},{2,1},{3,2},{4,3},{5,4},{6,5},{7,6},{8,7},{9,8},{10,9... | collective-permute-start | bytes 1032200 | tf_op jit(solution)/shard_map/ppermute | solution.py:23
  108.2 2.1 collective-permute-start.16
  111.9 0.8 constant_dynamic-update-slice_fusion.1
  112.7 6.8 %collective-permute-done.16 = f32[3,7,16,256]{3,2,1,0:T(8,128)S(1)} collective-permute-done((f32[3,7,16,256]{3,2,1,0:T(8,128)S(1)}, f32[3,7,16,256]{3,2,1,0:T(8,128)S(1)}, u32[]{:S(2)}, u32[]{:S(2)}) %collective-permute-start.16) | collective-permute-done | bytes 344096 | tf_op jit(solution)/shard_map/ppermute | solution.py:18
  120.3 4.3 %fusion.16 = f32[3,7,16,256]{3,2,1,0:T(8,128)S(1)} fusion(f32[3,7,16,7,256]{4,2,3,1,0:T(8,128)S(1)} %fusion.68, f32[3,7,256,256]{3,2,1,0:T(8,128)} %constant_dynamic-update-slice_fusion, f32[3,7]{1,0:T(4,128)S(1)} %compare_convert_fusion), kind=kOutput, calls=%fused_computation.15 | convolution fusion | flops 926306304 | bytes 8257620 | tf_op jit(solution)/shard_map/ibcas,iasr->ibcr/dot_general | solution.py:86
  124.6 7.0 %collective-permute-start.17 = (f32[15,16,256]{2,1,0:T(8,128)S(1)}, f32[15,16,256]{2,1,0:T(8,128)S(1)}, u32[]{:S(2)}, u32[]{:S(2)}) collective-permute-start(f32[15,16,256]{2,1,0:T(8,128)S(1)} %pad_maximum_fusion.2), channel_id=1, source_target_pairs={{0,16},{16,32},{32,48},{48,64},{64,80},{80,96},{96,112},{112,128},... | collective-permute-start | bytes 737288 | tf_op jit(solution)/shard_map/ppermute | solution.py:32
  131.6 3.1 %collective-permute-done.17 = f32[15,16,256]{2,1,0:T(8,128)S(1)} collective-permute-done((f32[15,16,256]{2,1,0:T(8,128)S(1)}, f32[15,16,256]{2,1,0:T(8,128)S(1)}, u32[]{:S(2)}, u32[]{:S(2)}) %collective-permute-start.17) | collective-permute-done | bytes 245792 | tf_op jit(solution)/shard_map/ppermute | solution.py:32
  135.0 3.5 %collective-permute-done.18 = f32[15,16,256]{2,1,0:T(8,128)S(1)} collective-permute-done((f32[15,16,256]{2,1,0:T(8,128)S(1)}, f32[15,16,256]{2,1,0:T(8,128)S(1)}, u32[]{:S(2)}, u32[]{:S(2)}) %collective-permute-start.18) | collective-permute-done | bytes 245792 | tf_op jit(solution)/shard_map/ppermute | solution.py:32
  138.7 4.3 %fusion.2 = f32[3,7,16,256,1]{3,2,0,1,4:T(8,128)S(1)} fusion(f32[3,7,16,7,256]{4,2,1,0,3:T(8,128)S(1)} %fusion.58, f32[3,7,256,256]{3,2,1,0:T(8,128)} %constant_dynamic-update-slice_fusion, f32[3,7]{1,0:T(4,128)S(1)} %compare_convert_fusion), kind=kOutput, calls=%fused_computation.2 | convolution fusion | flops 926220288 | bytes 8257620 | tf_op jit(solution)/shard_map/ibcas,iasr->ibcr/dot_general | solution.py:86
  143.0 0.8 fusion.80
  143.8 0.9 slice_bitcast_fusion.18
  144.7 1.0 slice_bitcast_fusion.10
  145.7 1.0 slice_bitcast_fusion.2
  147.3 2.8 %collective-permute-done.19 = f32[15,16,256]{2,1,0:T(8,128)S(1)} collective-permute-done((f32[15,16,256]{2,1,0:T(8,128)S(1)}, f32[15,16,256]{2,1,0:T(8,128)S(1)}, u32[]{:S(2)}, u32[]{:S(2)}) %collective-permute-start.19) | collective-permute-done | bytes 245792 | tf_op jit(solution)/shard_map/ppermute | solution.py:32
  150.1 3.7 %collective-permute-done.20 = f32[15,16,256]{2,1,0:T(8,128)S(1)} collective-permute-done((f32[15,16,256]{2,1,0:T(8,128)S(1)}, f32[15,16,256]{2,1,0:T(8,128)S(1)}, u32[]{:S(2)}, u32[]{:S(2)}) %collective-permute-start.20) | collective-permute-done | bytes 245792 | tf_op jit(solution)/shard_map/ppermute | solution.py:32
  154.2 55.2 %all-gather.2.cloned.1.call-done = f32[3,7,256,256]{3,2,1,0:T(8,128)} async-done(((f32[3,7,16,256]{3,2,1,0:T(8,128)}), f32[3,7,256,256]{3,2,1,0:T(8,128)}) %all-gather.2.cloned.1.call-update) | async-done | bytes 5505040 | tf_op jit(solution)/shard_map/all_gather | solution.py:97
  209.5 4.4 %fusion.6 = f32[3,7,16,256,1]{3,2,0,1,4:T(8,128)S(1)} fusion(f32[3,7,16,7,256]{4,2,1,0,3:T(8,128)S(1)} %fusion.32, f32[3,7,256,256]{3,2,1,0:T(8,128)} %all-gather.2.cloned.1.call-done), kind=kOutput, calls=%fused_computation.6 | convolution fusion | flops 924844032 | bytes 8257536 | tf_op jit(solution)/shard_map/ibcas,iasr->ibcr/dot_general | solution.py:86
  214.1 3.1 %collective-permute-start.21 = (f32[15,16,256]{2,1,0:T(8,128)S(1)}, f32[15,16,256]{2,1,0:T(8,128)S(1)}, u32[]{:S(2)}, u32[]{:S(2)}) collective-permute-start(f32[15,16,256]{2,1,0:T(8,128)S(1)} %pad_maximum_fusion.6), channel_id=1, source_target_pairs={{0,16},{16,32},{32,48},{48,64},{64,80},{80,96},{96,112},{112,128},... | collective-permute-start | bytes 737288 | tf_op jit(solution)/shard_map/ppermute | solution.py:32
  217.2 3.1 %collective-permute-done.21 = f32[15,16,256]{2,1,0:T(8,128)S(1)} collective-permute-done((f32[15,16,256]{2,1,0:T(8,128)S(1)}, f32[15,16,256]{2,1,0:T(8,128)S(1)}, u32[]{:S(2)}, u32[]{:S(2)}) %collective-permute-start.21) | collective-permute-done | bytes 245792 | tf_op jit(solution)/shard_map/ppermute | solution.py:32
  220.6 3.4 %collective-permute-done.22 = f32[15,16,256]{2,1,0:T(8,128)S(1)} collective-permute-done((f32[15,16,256]{2,1,0:T(8,128)S(1)}, f32[15,16,256]{2,1,0:T(8,128)S(1)}, u32[]{:S(2)}, u32[]{:S(2)}) %collective-permute-start.22) | collective-permute-done | bytes 245792 | tf_op jit(solution)/shard_map/ppermute | solution.py:32
  224.3 1.8 fusion.4
  226.0 0.9 fusion.78
  (128 shorter events, 12.4 us)
Async XLA Ops:
  6.5 202.9 %all-gather.2.cloned.1.call-start = ((), (), s32[]{:S(2)}) async-start(), calls=%async_computation | async-start | bytes 5849088 | tf_op jit(solution)/shard_map/all_gather | solution.py:97
  7.3 3.0 %copy-start.1 = (f32[3,7,16,256]{3,2,1,0:T(8,128)S(1)}, f32[3,7,16,256]{3,2,1,0:T(8,128)}, u32[]{:S(2)}) copy-start(f32[3,7,16,256]{3,2,1,0:T(8,128)} %param.2) | copy-start | bytes 1032196
  11.2 12.5 %collective-permute-start = (f32[15,16,256]{2,1,0:T(8,128)S(1)}, f32[15,16,256]{2,1,0:T(8,128)S(1)}, u32[]{:S(2)}, u32[]{:S(2)}) collective-permute-start(f32[15,16,256]{2,1,0:T(8,128)S(1)} %pad_maximum_fusion), channel_id=1, source_target_pairs={{0,16},{16,32},{32,48},{48,64},{64,80},{80,96},{96,112},{112,128},... | collective-permute-start | bytes 737288 | tf_op jit(solution)/shard_map/ppermute | solution.py:32
  14.7 12.7 %collective-permute-start.2 = (f32[3,7,16,256]{3,2,1,0:T(8,128)S(1)}, f32[3,7,16,256]{3,2,1,0:T(8,128)S(1)}, u32[]{:S(2)}, u32[]{:S(2)}) collective-permute-start(f32[3,7,16,256]{3,2,1,0:T(8,128)S(1)} %copy-done.1), channel_id=1, source_target_pairs={{0,1},{1,2},{2,3},{3,4},{4,5},{5,6},{6,7},{7,8},{8,9},{9,10},{10,1... | collective-permute-start | bytes 1032200 | tf_op jit(solution)/shard_map/ppermute | solution.py:18
  17.8 12.5 %collective-permute-start.3 = (f32[3,7,16,256]{3,2,1,0:T(8,128)S(1)}, f32[3,7,16,256]{3,2,1,0:T(8,128)S(1)}, u32[]{:S(2)}, u32[]{:S(2)}) collective-permute-start(f32[3,7,16,256]{3,2,1,0:T(8,128)S(1)} %copy-done.1), channel_id=1, source_target_pairs={{0,15},{1,0},{2,1},{3,2},{4,3},{5,4},{6,5},{7,6},{8,7},{9,8},{10,9... | collective-permute-start | bytes 1032200 | tf_op jit(solution)/shard_map/ppermute | solution.py:23
  23.4 12.9 %copy-start.2 = (pred[7]{0:T(512)(128)(4,1)S(1)}, pred[7]{0:T(512)(128)(4,1)}, u32[]{:S(2)}) copy-start(pred[7]{0:T(512)(128)(4,1)} %constant.104.clone.1) | copy-start | bytes 25
  23.4 6.8 %collective-permute-start.1 = (f32[15,16,256]{2,1,0:T(8,128)S(1)}, f32[15,16,256]{2,1,0:T(8,128)S(1)}, u32[]{:S(2)}, u32[]{:S(2)}) collective-permute-start(f32[15,16,256]{2,1,0:T(8,128)S(1)} %pad_maximum_fusion.1), channel_id=1, source_target_pairs={{0,496},{16,0},{32,16},{48,32},{64,48},{80,64},{96,80},{112,96},{1... | collective-permute-start | bytes 737288 | tf_op jit(solution)/shard_map/ppermute | solution.py:32
  27.4 13.7 %collective-permute-start.4 = (f32[3,7,16,256]{3,2,1,0:T(8,128)S(1)}, f32[3,7,16,256]{3,2,1,0:T(8,128)S(1)}, u32[]{:S(2)}, u32[]{:S(2)}) collective-permute-start(f32[3,7,16,256]{3,2,1,0:T(8,128)S(1)} %collective-permute-done.2), channel_id=1, source_target_pairs={{0,1},{1,2},{2,3},{3,4},{4,5},{5,6},{6,7},{7,8},{8,9},{9,10},{10,1... | collective-permute-start | bytes 1032200 | tf_op jit(solution)/shard_map/ppermute | solution.py:18
  30.3 12.8 %collective-permute-start.5 = (f32[3,7,16,256]{3,2,1,0:T(8,128)S(1)}, f32[3,7,16,256]{3,2,1,0:T(8,128)S(1)}, u32[]{:S(2)}, u32[]{:S(2)}) collective-permute-start(f32[3,7,16,256]{3,2,1,0:T(8,128)S(1)} %collective-permute-done.3), channel_id=1, source_target_pairs={{0,15},{1,0},{2,1},{3,2},{4,3},{5,4},{6,5},{7,6},{8,7},{9,8},{10,9... | collective-permute-start | bytes 1032200 | tf_op jit(solution)/shard_map/ppermute | solution.py:23
  41.1 14.9 %collective-permute-start.6 = (f32[3,7,16,256]{3,2,1,0:T(8,128)S(1)}, f32[3,7,16,256]{3,2,1,0:T(8,128)S(1)}, u32[]{:S(2)}, u32[]{:S(2)}) collective-permute-start(f32[3,7,16,256]{3,2,1,0:T(8,128)S(1)} %collective-permute-done.4), channel_id=1, source_target_pairs={{0,1},{1,2},{2,3},{3,4},{4,5},{5,6},{6,7},{7,8},{8,9},{9,10},{10,1... | collective-permute-start | bytes 1032200 | tf_op jit(solution)/shard_map/ppermute | solution.py:18
  43.1 15.6 %collective-permute-start.7 = (f32[3,7,16,256]{3,2,1,0:T(8,128)S(1)}, f32[3,7,16,256]{3,2,1,0:T(8,128)S(1)}, u32[]{:S(2)}, u32[]{:S(2)}) collective-permute-start(f32[3,7,16,256]{3,2,1,0:T(8,128)S(1)} %collective-permute-done.5), channel_id=1, source_target_pairs={{0,15},{1,0},{2,1},{3,2},{4,3},{5,4},{6,5},{7,6},{8,7},{9,8},{10,9... | collective-permute-start | bytes 1032200 | tf_op jit(solution)/shard_map/ppermute | solution.py:23
  56.0 14.4 %collective-permute-start.8 = (f32[3,7,16,256]{3,2,1,0:T(8,128)S(1)}, f32[3,7,16,256]{3,2,1,0:T(8,128)S(1)}, u32[]{:S(2)}, u32[]{:S(2)}) collective-permute-start(f32[3,7,16,256]{3,2,1,0:T(8,128)S(1)} %collective-permute-done.6), channel_id=1, source_target_pairs={{0,1},{1,2},{2,3},{3,4},{4,5},{5,6},{6,7},{7,8},{8,9},{9,10},{10,1... | collective-permute-start | bytes 1032200 | tf_op jit(solution)/shard_map/ppermute | solution.py:18
  58.7 15.2 %collective-permute-start.9 = (f32[3,7,16,256]{3,2,1,0:T(8,128)S(1)}, f32[3,7,16,256]{3,2,1,0:T(8,128)S(1)}, u32[]{:S(2)}, u32[]{:S(2)}) collective-permute-start(f32[3,7,16,256]{3,2,1,0:T(8,128)S(1)} %collective-permute-done.7), channel_id=1, source_target_pairs={{0,15},{1,0},{2,1},{3,2},{4,3},{5,4},{6,5},{7,6},{8,7},{9,8},{10,9... | collective-permute-start | bytes 1032200 | tf_op jit(solution)/shard_map/ppermute | solution.py:23
  70.4 13.5 %collective-permute-start.10 = (f32[3,7,16,256]{3,2,1,0:T(8,128)S(1)}, f32[3,7,16,256]{3,2,1,0:T(8,128)S(1)}, u32[]{:S(2)}, u32[]{:S(2)}) collective-permute-start(f32[3,7,16,256]{3,2,1,0:T(8,128)S(1)} %collective-permute-done.8), channel_id=1, source_target_pairs={{0,1},{1,2},{2,3},{3,4},{4,5},{5,6},{6,7},{7,8},{8,9},{9,10},{10,1... | collective-permute-start | bytes 1032200 | tf_op jit(solution)/shard_map/ppermute | solution.py:18
  73.9 13.5 %collective-permute-start.11 = (f32[3,7,16,256]{3,2,1,0:T(8,128)S(1)}, f32[3,7,16,256]{3,2,1,0:T(8,128)S(1)}, u32[]{:S(2)}, u32[]{:S(2)}) collective-permute-start(f32[3,7,16,256]{3,2,1,0:T(8,128)S(1)} %collective-permute-done.9), channel_id=1, source_target_pairs={{0,15},{1,0},{2,1},{3,2},{4,3},{5,4},{6,5},{7,6},{8,7},{9,8},{10,9... | collective-permute-start | bytes 1032200 | tf_op jit(solution)/shard_map/ppermute | solution.py:23
  83.9 12.6 %collective-permute-start.12 = (f32[3,7,16,256]{3,2,1,0:T(8,128)S(1)}, f32[3,7,16,256]{3,2,1,0:T(8,128)S(1)}, u32[]{:S(2)}, u32[]{:S(2)}) collective-permute-start(f32[3,7,16,256]{3,2,1,0:T(8,128)S(1)} %collective-permute-done.10), channel_id=1, source_target_pairs={{0,1},{1,2},{2,3},{3,4},{4,5},{5,6},{6,7},{7,8},{8,9},{9,10},{10,1... | collective-permute-start | bytes 1032200 | tf_op jit(solution)/shard_map/ppermute | solution.py:18
  87.4 12.6 %collective-permute-start.13 = (f32[3,7,16,256]{3,2,1,0:T(8,128)S(1)}, f32[3,7,16,256]{3,2,1,0:T(8,128)S(1)}, u32[]{:S(2)}, u32[]{:S(2)}) collective-permute-start(f32[3,7,16,256]{3,2,1,0:T(8,128)S(1)} %collective-permute-done.11), channel_id=1, source_target_pairs={{0,15},{1,0},{2,1},{3,2},{4,3},{5,4},{6,5},{7,6},{8,7},{9,8},{10,9... | collective-permute-start | bytes 1032200 | tf_op jit(solution)/shard_map/ppermute | solution.py:23
  96.5 11.7 %collective-permute-start.14 = (f32[3,7,16,256]{3,2,1,0:T(8,128)S(1)}, f32[3,7,16,256]{3,2,1,0:T(8,128)S(1)}, u32[]{:S(2)}, u32[]{:S(2)}) collective-permute-start(f32[3,7,16,256]{3,2,1,0:T(8,128)S(1)} %collective-permute-done.12), channel_id=1, source_target_pairs={{0,1},{1,2},{2,3},{3,4},{4,5},{5,6},{6,7},{7,8},{8,9},{9,10},{10,1... | collective-permute-start | bytes 1032200 | tf_op jit(solution)/shard_map/ppermute | solution.py:18
  100.0 11.9 %collective-permute-start.15 = (f32[3,7,16,256]{3,2,1,0:T(8,128)S(1)}, f32[3,7,16,256]{3,2,1,0:T(8,128)S(1)}, u32[]{:S(2)}, u32[]{:S(2)}) collective-permute-start(f32[3,7,16,256]{3,2,1,0:T(8,128)S(1)} %collective-permute-done.13), channel_id=1, source_target_pairs={{0,15},{1,0},{2,1},{3,2},{4,3},{5,4},{6,5},{7,6},{8,7},{9,8},{10,9... | collective-permute-start | bytes 1032200 | tf_op jit(solution)/shard_map/ppermute | solution.py:23
  108.2 11.3 %collective-permute-start.16 = (f32[3,7,16,256]{3,2,1,0:T(8,128)S(1)}, f32[3,7,16,256]{3,2,1,0:T(8,128)S(1)}, u32[]{:S(2)}, u32[]{:S(2)}) collective-permute-start(f32[3,7,16,256]{3,2,1,0:T(8,128)S(1)} %collective-permute-done.14), channel_id=1, source_target_pairs={{0,1},{1,2},{2,3},{3,4},{4,5},{5,6},{6,7},{7,8},{8,9},{9,10},{10,1... | collective-permute-start | bytes 1032200 | tf_op jit(solution)/shard_map/ppermute | solution.py:18
  124.6 10.1 %collective-permute-start.17 = (f32[15,16,256]{2,1,0:T(8,128)S(1)}, f32[15,16,256]{2,1,0:T(8,128)S(1)}, u32[]{:S(2)}, u32[]{:S(2)}) collective-permute-start(f32[15,16,256]{2,1,0:T(8,128)S(1)} %pad_maximum_fusion.2), channel_id=1, source_target_pairs={{0,16},{16,32},{32,48},{48,64},{64,80},{80,96},{96,112},{112,128},... | collective-permute-start | bytes 737288 | tf_op jit(solution)/shard_map/ppermute | solution.py:32
  131.6 6.8 %collective-permute-start.18 = (f32[15,16,256]{2,1,0:T(8,128)S(1)}, f32[15,16,256]{2,1,0:T(8,128)S(1)}, u32[]{:S(2)}, u32[]{:S(2)}) collective-permute-start(f32[15,16,256]{2,1,0:T(8,128)S(1)} %pad_maximum_fusion.3), channel_id=1, source_target_pairs={{0,496},{16,0},{32,16},{48,32},{64,48},{80,64},{96,80},{112,96},{1... | collective-permute-start | bytes 737288 | tf_op jit(solution)/shard_map/ppermute | solution.py:32
  143.8 10.1 %copy-start = (f32[3,7,16,256]{3,2,1,0:T(8,128)S(1)}, f32[3,7,16,256]{3,2,1,0:T(8,128)}, u32[]{:S(2)}) copy-start(f32[3,7,16,256]{3,2,1,0:T(8,128)} %fusion.80) | copy-start | bytes 1032196
  146.7 3.4 %collective-permute-start.19 = (f32[15,16,256]{2,1,0:T(8,128)S(1)}, f32[15,16,256]{2,1,0:T(8,128)S(1)}, u32[]{:S(2)}, u32[]{:S(2)}) collective-permute-start(f32[15,16,256]{2,1,0:T(8,128)S(1)} %pad_maximum_fusion.4), channel_id=1, source_target_pairs={{0,16},{16,32},{32,48},{48,64},{64,80},{80,96},{96,112},{112,128},... | collective-permute-start | bytes 737288 | tf_op jit(solution)/shard_map/ppermute | solution.py:32
  147.0 6.8 %collective-permute-start.20 = (f32[15,16,256]{2,1,0:T(8,128)S(1)}, f32[15,16,256]{2,1,0:T(8,128)S(1)}, u32[]{:S(2)}, u32[]{:S(2)}) collective-permute-start(f32[15,16,256]{2,1,0:T(8,128)S(1)} %pad_maximum_fusion.5), channel_id=1, source_target_pairs={{0,496},{16,0},{32,16},{48,32},{64,48},{80,64},{96,80},{112,96},{1... | collective-permute-start | bytes 737288 | tf_op jit(solution)/shard_map/ppermute | solution.py:32
  209.5 14.8 %slice-start = ((s8[5505024]{0:T(1024)(128)(4,1)}), s8[4194304]{0:T(1024)(128)(4,1)S(1)}, s32[]{:S(2)}) async-start(s8[5505024]{0:T(1024)(128)(4,1)} %bitcast.255), calls=%async_computation.1 | async-start | bytes 8388608
  214.0 10.3 %slice-start.1 = ((s8[5505024]{0:T(1024)(128)(4,1)}), s8[1310720]{0:T(1024)(128)(4,1)S(1)}, s32[]{:S(2)}) async-start(s8[5505024]{0:T(1024)(128)(4,1)} %bitcast.255), calls=%async_computation.2 | async-start | bytes 2621440
  214.1 6.2 %collective-permute-start.21 = (f32[15,16,256]{2,1,0:T(8,128)S(1)}, f32[15,16,256]{2,1,0:T(8,128)S(1)}, u32[]{:S(2)}, u32[]{:S(2)}) collective-permute-start(f32[15,16,256]{2,1,0:T(8,128)S(1)} %pad_maximum_fusion.6), channel_id=1, source_target_pairs={{0,16},{16,32},{32,48},{48,64},{64,80},{80,96},{96,112},{112,128},... | collective-permute-start | bytes 737288 | tf_op jit(solution)/shard_map/ppermute | solution.py:32
  217.2 6.8 %collective-permute-start.22 = (f32[15,16,256]{2,1,0:T(8,128)S(1)}, f32[15,16,256]{2,1,0:T(8,128)S(1)}, u32[]{:S(2)}, u32[]{:S(2)}) collective-permute-start(f32[15,16,256]{2,1,0:T(8,128)S(1)} %pad_maximum_fusion.7), channel_id=1, source_target_pairs={{0,496},{16,0},{32,16},{48,32},{64,48},{80,64},{96,80},{112,96},{1... | collective-permute-start | bytes 737288 | tf_op jit(solution)/shard_map/ppermute | solution.py:32
Sparse Core Ops, SparseCore 0:
  143.9 65.4 all-gather.1
